TPU v7x, 256 devices: a whole 4x4x8 slice. The times are simulated.
256 devices in a mesh: dp: 32 (over x, z_hi, y), owner: 8 (over z_lo, core).
Axes of the slice: x: 4, y: 4, z: 8 (z_hi: 2, z_lo: 4; z = z_hi * 4 + z_lo), core: 2. Of those that a mesh axis runs over, the one named last changes fastest.
Arguments:
- line_columns: bfloat16 [8, 131072, 512], P(None, ('dp', 'owner')), may hold values from -12 to 12
- line_widths: int32 [256, 4], P(('dp', 'owner')), may hold values from 1 to 128, as said below
- layer_owner: int32 [8], replicated, may hold values from 0 to 7, each once
Outputs:
- preconditioned: float32 [8, 1152, 128], replicated
Inputs may be any that keep to these rules, and one draw needn't show every extreme that they name: `line_widths`: row b holds the widths of the 4 lines of device b, laid end to end from its first position; in every draw the lines of some device all have width 128.
All inputs are finite; a program needn't handle non-finite values.
Results may differ from a plain program's by a relative error of at most 0.0003.
Values may be sent and summed in bfloat16 or wider, within the bound.
No kernel may reach another device: no remote copies, remote signals or barrier semaphores. Data moves between devices by JAX's collectives and lax.ppermute only.
A program may use at most 128 MiB of HBM per device.

v0:
```python
import numpy as np
import jax
import jax.numpy as jnp
from jax import lax
from jax.sharding import PartitionSpec as P

damping = 0.1


def patch_columns(block, widths):
    positions = block.shape[-2]
    channels = block.shape[-1] // 4
    line_ends = jnp.cumsum(widths, axis=-1).astype(jnp.int32)
    line_starts = line_ends - widths
    place = jnp.arange(positions, dtype=jnp.int32)[:, None]
    opening = jnp.any(place == line_starts[..., None, :], axis=-1)[..., None]
    closing = jnp.any(place + 1 == line_ends[..., None, :], axis=-1)[..., None]
    inside = place < line_ends[..., None, -1:]
    features = block[..., : 3 * channels]
    gradients = block[..., 3 * channels :]
    padding = jnp.zeros_like(features[..., :1, :])
    before = jnp.concatenate([padding, features[..., :-1, :]], axis=-2)
    after = jnp.concatenate([features[..., 1:, :], padding], axis=-2)
    before = jnp.where(opening, jnp.zeros_like(before), before)
    after = jnp.where(closing, jnp.zeros_like(after), after)
    stacked = jnp.concatenate([before, features, after, gradients], axis=-1)
    return jnp.where(inside, stacked, jnp.zeros_like(stacked))


def precondition(factor, total_rows):
    full_width = factor.shape[0]
    patch_width = full_width // 10 * 9
    scaled = factor / total_rows
    act_factor = scaled[:patch_width, :patch_width] + damping * jnp.eye(
        patch_width, dtype=factor.dtype
    )
    grad_factor = scaled[patch_width:, patch_width:] + damping * jnp.eye(
        full_width - patch_width, dtype=factor.dtype
    )
    cross_term = scaled[:patch_width, patch_width:]
    act_cholesky = jnp.linalg.cholesky(act_factor)
    left_solved = jax.scipy.linalg.cho_solve((act_cholesky, True), cross_term)
    grad_cholesky = jnp.linalg.cholesky(grad_factor)
    return jax.scipy.linalg.cho_solve((grad_cholesky, True), left_solved.T).T


def _tri_pairs(nb):
    return [(i, j) for i in range(nb) for j in range(i + 1)]


def pack_lower(gram, block):
    nb = gram.shape[0] // block
    tiles = gram.reshape(nb, block, nb, block).transpose(0, 2, 1, 3)
    pairs = _tri_pairs(nb)
    rows = np.array([p[0] for p in pairs], dtype=np.int32)
    cols = np.array([p[1] for p in pairs], dtype=np.int32)
    return tiles[rows, cols]


def unpack_lower(blocks, nb):
    block = blocks.shape[-1]
    index = {p: k for k, p in enumerate(_tri_pairs(nb))}
    pick = np.array(
        [[index[max(i, j), min(i, j)] for j in range(nb)] for i in range(nb)], dtype=np.int32
    )
    upper = np.array([[i < j for j in range(nb)] for i in range(nb)])
    tiles = blocks[pick]
    tiles = jnp.where(upper[:, :, None, None], jnp.swapaxes(tiles, -1, -2), tiles)
    return tiles.transpose(0, 2, 1, 3).reshape(nb * block, nb * block)


HIGH = lax.Precision.HIGHEST


def _mm(a, b):
    return jnp.dot(a, b, precision=HIGH, preferred_element_type=jnp.float32)


def _mm_t(a, b):
    return lax.dot_general(
        a, b, (((0,), (0,)), ((), ())), precision=HIGH, preferred_element_type=jnp.float32
    )


def _mm_nt(a, b):
    return lax.dot_general(
        a, b, (((1,), (1,)), ((), ())), precision=HIGH, preferred_element_type=jnp.float32
    )


def _chol_inv(block):
    lower = jnp.linalg.cholesky(block, symmetrize_input=False)
    eye = jnp.eye(block.shape[0], dtype=block.dtype)
    inverse = lax.linalg.triangular_solve(lower, eye, left_side=True, lower=True)
    return (lower, inverse)


def precondition_blocks(blocks, nb, total_rows):
    block = blocks.shape[-1]
    na = nb - 1
    index = {p: k for k, p in enumerate(_tri_pairs(nb))}
    zero = len(index)
    pick = np.array(
        [[index[i, j] if i >= j else zero for j in range(na)] for i in range(nb)], dtype=np.int32
    )
    scale = 1.0 / total_rows
    tiles = blocks[pick] * scale
    work = tiles.transpose(0, 2, 1, 3).reshape(nb * block, na * block)
    eye = jnp.eye(block, dtype=blocks.dtype)
    grad_factor = blocks[index[na, na]] * scale + damping * eye
    inverses = []
    for k in range(na):
        lo = k * block
        hi = lo + block
        diag = work[lo:hi, lo:hi] + damping * eye
        lower, inverse = _chol_inv(diag)
        inverses.append(inverse)
        panel = _mm_nt(work[hi:, lo:hi], inverse)
        work = work.at[lo:hi, lo:hi].set(lower)
        work = work.at[hi:, lo:hi].set(panel)
        if k + 1 < na:
            update = _mm_nt(panel, panel[: (na - k - 1) * block])
            work = work.at[hi:, hi:].add(-update)
    solved_t = work[na * block :, :]
    pieces = [None] * na
    for k in reversed(range(na)):
        lo = k * block
        hi = lo + block
        rhs = solved_t[:, lo:hi].T
        if k + 1 < na:
            below = jnp.concatenate(pieces[k + 1 :], axis=0)
            rhs = rhs - _mm_t(work[hi : na * block, lo:hi], below)
        pieces[k] = _mm_t(inverses[k], rhs)
    left_solved = jnp.concatenate(pieces, axis=0)
    _, grad_inverse = _chol_inv(grad_factor)
    return _mm(_mm_nt(left_solved, grad_inverse), grad_inverse)


def body(line_columns, line_widths, layer_owner):
    layer_count, positions, packed_width = line_columns.shape
    channels = packed_width // 4
    full_width = 10 * channels
    n_replicas = 1
    for axis in DP_AXES:
        n_replicas = n_replicas * lax.axis_size(axis)
    n_owners = lax.axis_size("owner")
    per_owner = layer_count // n_owners
    total_rows = n_replicas * n_owners * positions
    ordered = jnp.take(line_columns, layer_owner, axis=0)
    width_copies = jnp.broadcast_to(line_widths[None, :, :], (n_owners, 1, line_widths.shape[1]))
    received, source_widths = (
        lax.all_to_all(ordered, "owner", split_axis=0, concat_axis=1, tiled=True),
        lax.all_to_all(width_copies, "owner", split_axis=0, concat_axis=1, tiled=True),
    )
    blocks = received.reshape(per_owner, n_owners, positions, packed_width)
    columns = patch_columns(blocks, source_widths.reshape(n_owners, line_widths.shape[1]))
    columns = columns.reshape(n_owners * positions, full_width)
    gram = jnp.dot(columns.T, columns, preferred_element_type=jnp.float32)
    block = 128
    nb = full_width // block
    packed = pack_lower(gram, block)
    n_blocks = packed.shape[0]
    padded = -(-n_blocks * block // (8 * n_replicas)) * 8 * n_replicas // block
    packed = jnp.concatenate(
        [packed, jnp.zeros((padded - n_blocks, block, block), packed.dtype)], axis=0
    )
    chunk = padded * block // n_replicas
    packed = packed.reshape(n_replicas, chunk, block)
    mine = packed.reshape(padded * block, block)
    for axis in SCATTER_ORDER:
        mine = lax.psum_scatter(mine, axis, scatter_dimension=0, tiled=True)
    gathered = mine
    for axis in SCATTER_ORDER[::-1]:
        gathered = lax.all_gather(gathered, axis, axis=0, tiled=True)
    gathered = gathered.reshape(padded, block, block)
    results = precondition_blocks(gathered, nb, total_rows)[None]
    return lax.all_gather(results, "owner", axis=0, tiled=True)


DP_AXES = ("dp_x", "dp_z", "dp_y")
SCATTER_ORDER = ("dp_y", "dp_x", "dp_z")


def solution(mesh):
    dp_shape = (4, 2, mesh.shape["dp"] // 8)
    devices = mesh.devices.reshape(dp_shape + (mesh.shape["owner"],))
    fine = jax.sharding.Mesh(devices, DP_AXES + ("owner",))
    rows = DP_AXES + ("owner",)
    in_specs = (P(None, rows, None), P(rows, None), P())
    out_specs = P()
    return jax.shard_map(body, mesh=fine, in_specs=in_specs, out_specs=out_specs, check_vma=False)
```

profile of v0, /device:TPU:2, one launch (start us, length us, event | category | flops | bytes accessed | tf_op | source)
XLA Modules:
  0.0 770.8 jit_solution(15448216205919539234)
XLA Ops:
  30.2 93.7 %all-to-all-done.1 = bf16[8,512,512]{2,1,0:T(8,128)(2,1)} async-done(((bf16[8,512,512]{2,1,0:T(8,128)(2,1)}), bf16[8,512,512]{2,1,0:T(8,128)(2,1)}, u32[]{:S(2)}, u32[]{:S(2)}) %all-to-all-start.1) | async-done | bytes 4194336 | tf_op jit(solution)/shard_map/all_to_all | solution.py:152
  139.5 14.3 %copy.37 = bf16[1280,4096]{1,0:T(8,128)(2,1)} copy(bf16[1280,4096]{0,1:T(8,128)(2,1)} %fusion) | data formatting | bytes 20971520 | tf_op jit(solution)/shard_map/dot_general | solution.py:158
  153.9 22.7 %convolution_bitcast_fusion = f32[10,10,128,128]{3,2,1,0:T(8,128)} fusion(bf16[10,128,4096,1]{2,1,3,0:T(8,128)(2,1)} %bitcast.176, bf16[10,128,4096,1]{2,1,0,3:T(8,128)(2,1)} %bitcast.177), kind=kOutput, calls=%fused_computation.13 | convolution fusion | flops 13421772800 | bytes 27525120 | tf_op jit(solution)/shard_map/dot_general | solution.py:158
  186.4 45.5 %reduce-scatter.4.cloned.1.call-done = f32[1792,128]{1,0:T(8,128)} async-done(((f32[7168,128]{1,0:T(8,128)}), f32[1792,128]{1,0:T(8,128)}) %reduce-scatter.4.cloned.1.call-update) | async-done | bytes 917520 | tf_op jit(solution)/shard_map/reduce_scatter | solution.py:171
  232.1 25.5 %reduce-scatter.6.cloned.1.call-done = f32[448,128]{1,0:T(8,128)} async-done(((f32[1792,128]{1,0:T(8,128)}), f32[448,128]{1,0:T(8,128)}) %reduce-scatter.6.cloned.1.call-update) | async-done | bytes 229392 | tf_op jit(solution)/shard_map/reduce_scatter | solution.py:171
  257.6 27.6 %reduce-scatter.8.cloned.1.call-done = f32[224,128]{1,0:T(8,128)} async-done(((f32[448,128]{1,0:T(8,128)}), f32[224,128]{1,0:T(8,128)}) %reduce-scatter.8.cloned.1.call-update) | async-done | bytes 114704 | tf_op jit(solution)/shard_map/reduce_scatter | solution.py:171
  285.2 12.2 %all_gather.12 = f32[448,128]{1,0:T(8,128)S(1)} all-gather(f32[224,128]{1,0:T(8,128)} %reduce-scatter.8.cloned.1.call-done), channel_id=1, replica_groups=mesh['dp_x'=4,'dp_z'=2,'dp_y'=4,'owner'=8] {'dp_z'}, dimensions={0}, use_global_device_ids=true | all-gather | bytes 344064 | tf_op jit(solution)/shard_map/all_gather | solution.py:174
  297.4 14.3 %all_gather.13 = f32[1792,128]{1,0:T(8,128)} all-gather(f32[448,128]{1,0:T(8,128)S(1)} %all_gather.12), channel_id=1, replica_groups=mesh['dp_x'=4,'dp_z'=2,'dp_y'=4,'owner'=8] {'dp_x'}, dimensions={0}, use_global_device_ids=true | all-gather | bytes 1146880 | tf_op jit(solution)/shard_map/all_gather | solution.py:174
  311.8 43.0 %all-gather.4.cloned.1.call-done = f32[7168,128]{1,0:T(8,128)} async-done(((f32[1792,128]{1,0:T(8,128)}), f32[7168,128]{1,0:T(8,128)}) %all-gather.4.cloned.1.call-update) | async-done | bytes 3670032 | tf_op jit(solution)/shard_map/all_gather | solution.py:174
  366.6 9.8 %copy.38 = f32[10,128,9,128]{1,0,3,2:T(8,128)} copy(f32[10,128,9,128]{3,1,2,0:T(8,128)} %bitcast.171) | data formatting | bytes 11796480 | tf_op jit(solution)/shard_map/mul | solution.py:107
  376.5 9.2 %copy.61 = f32[144,8,10,128]{3,1,2,0:T(8,128)} copy(f32[144,8,10,128]{3,2,1,0:T(8,128)} %bitcast.168) | data formatting | bytes 11796480
  394.2 11.7 %cholesky.165 = f32[128,128]{1,0:T(8,128)S(1)} custom-call(f32[128,128]{1,0:T(8,128)S(1)} %select_add_fusion.9), custom_call_target="Cholesky" | custom-call | tf_op jit(solution)/shard_map/jit(cholesky)/cholesky | solution.py:92
  407.9 9.8 %custom-call.16 = f32[1,128,128]{1,2,0:T(8,128)S(1)} custom-call(f32[1,128,128]{2,1,0:T(8,128)S(1)} %get-tuple-element.334), custom_call_target="InvertDiagBlocksLowerTriangular" | custom-call | tf_op jit(solution)/shard_map/triangular_solve/custom-call.0 | solution.py:94
  430.9 11.7 %cholesky.176 = f32[128,128]{1,0:T(8,128)S(1)} custom-call(f32[128,128]{1,0:T(8,128)S(1)} %select_add_fusion.8), custom_call_target="Cholesky" | custom-call | tf_op jit(solution)/shard_map/jit(cholesky)/cholesky | solution.py:92
  444.7 9.8 %custom-call.17 = f32[1,128,128]{1,2,0:T(8,128)S(1)} custom-call(f32[1,128,128]{2,1,0:T(8,128)S(1)} %get-tuple-element.332), custom_call_target="InvertDiagBlocksLowerTriangular" | custom-call | tf_op jit(solution)/shard_map/triangular_solve/custom-call.0 | solution.py:94
  465.4 11.7 %cholesky.187 = f32[128,128]{1,0:T(8,128)S(1)} custom-call(f32[128,128]{1,0:T(8,128)S(1)} %select_add_fusion.7), custom_call_target="Cholesky" | custom-call | tf_op jit(solution)/shard_map/jit(cholesky)/cholesky | solution.py:92
  479.2 9.8 %custom-call.18 = f32[1,128,128]{1,2,0:T(8,128)S(1)} custom-call(f32[1,128,128]{2,1,0:T(8,128)S(1)} %get-tuple-element.330), custom_call_target="InvertDiagBlocksLowerTriangular" | custom-call | tf_op jit(solution)/shard_map/triangular_solve/custom-call.0 | solution.py:94
  497.5 11.9 %cholesky.198 = f32[128,128]{1,0:T(8,128)S(1)} custom-call(f32[128,128]{1,0:T(8,128)S(1)} %select_add_fusion.6), custom_call_target="Cholesky" | custom-call | tf_op jit(solution)/shard_map/jit(cholesky)/cholesky | solution.py:92
  511.3 9.8 %custom-call.19 = f32[1,128,128]{1,2,0:T(8,128)S(1)} custom-call(f32[1,128,128]{2,1,0:T(8,128)S(1)} %get-tuple-element.328), custom_call_target="InvertDiagBlocksLowerTriangular" | custom-call | tf_op jit(solution)/shard_map/triangular_solve/custom-call.0 | solution.py:94
  527.4 11.7 %cholesky.209 = f32[128,128]{1,0:T(8,128)S(1)} custom-call(f32[128,128]{1,0:T(8,128)S(1)} %select_add_fusion.5), custom_call_target="Cholesky" | custom-call | tf_op jit(solution)/shard_map/jit(cholesky)/cholesky | solution.py:92
  541.1 9.8 %custom-call.20 = f32[1,128,128]{1,2,0:T(8,128)S(1)} custom-call(f32[1,128,128]{2,1,0:T(8,128)S(1)} %get-tuple-element.326), custom_call_target="InvertDiagBlocksLowerTriangular" | custom-call | tf_op jit(solution)/shard_map/triangular_solve/custom-call.0 | solution.py:94
  556.6 11.7 %cholesky.220 = f32[128,128]{1,0:T(8,128)S(1)} custom-call(f32[128,128]{1,0:T(8,128)S(1)} %select_add_fusion.4), custom_call_target="Cholesky" | custom-call | tf_op jit(solution)/shard_map/jit(cholesky)/cholesky | solution.py:92
  570.2 9.8 %custom-call.21 = f32[1,128,128]{1,2,0:T(8,128)S(1)} custom-call(f32[1,128,128]{2,1,0:T(8,128)S(1)} %get-tuple-element.323), custom_call_target="InvertDiagBlocksLowerTriangular" | custom-call | tf_op jit(solution)/shard_map/triangular_solve/custom-call.0 | solution.py:94
  585.3 11.9 %cholesky.264 = f32[128,128]{1,0:T(8,128)S(1)} custom-call(f32[128,128]{1,0:T(8,128)S(1)} %select_add_fusion), custom_call_target="Cholesky" | custom-call | tf_op jit(solution)/shard_map/jit(cholesky)/cholesky | solution.py:92
  598.5 9.8 %custom-call.25 = f32[1,128,128]{1,2,0:T(8,128)S(1)} custom-call(f32[1,128,128]{2,1,0:T(8,128)S(1)} %fusion.72), custom_call_target="InvertDiagBlocksLowerTriangular" | custom-call | tf_op jit(solution)/shard_map/triangular_solve/custom-call.0 | solution.py:94
  608.6 11.7 %cholesky.231 = f32[128,128]{1,0:T(8,128)S(1)} custom-call(f32[128,128]{1,0:T(8,128)S(1)} %select_add_fusion.3), custom_call_target="Cholesky" | custom-call | tf_op jit(solution)/shard_map/jit(cholesky)/cholesky | solution.py:92
  622.3 9.8 %custom-call.22 = f32[1,128,128]{1,2,0:T(8,128)S(1)} custom-call(f32[1,128,128]{2,1,0:T(8,128)S(1)} %get-tuple-element.321), custom_call_target="InvertDiagBlocksLowerTriangular" | custom-call | tf_op jit(solution)/shard_map/triangular_solve/custom-call.0 | solution.py:94
  634.9 11.9 %cholesky.242 = f32[128,128]{1,0:T(8,128)S(1)} custom-call(f32[128,128]{1,0:T(8,128)S(1)} %select_add_fusion.2), custom_call_target="Cholesky" | custom-call | tf_op jit(solution)/shard_map/jit(cholesky)/cholesky | solution.py:92
  648.2 9.8 %custom-call.23 = f32[1,128,128]{1,2,0:T(8,128)S(1)} custom-call(f32[1,128,128]{2,1,0:T(8,128)S(1)} %fusion.70), custom_call_target="InvertDiagBlocksLowerTriangular" | custom-call | tf_op jit(solution)/shard_map/triangular_solve/custom-call.0 | solution.py:94
  658.9 11.7 %cholesky.253 = f32[128,128]{1,0:T(8,128)S(1)} custom-call(f32[128,128]{1,0:T(8,128)S(1)} %select_add_fusion.1), custom_call_target="Cholesky" | custom-call | tf_op jit(solution)/shard_map/jit(cholesky)/cholesky | solution.py:92
  671.9 9.8 %custom-call.24 = f32[1,128,128]{1,2,0:T(8,128)S(1)} custom-call(f32[1,128,128]{2,1,0:T(8,128)S(1)} %fusion.71), custom_call_target="InvertDiagBlocksLowerTriangular" | custom-call | tf_op jit(solution)/shard_map/triangular_solve/custom-call.0 | solution.py:94
  698.9 60.0 %all-gather.6.cloned.1.call-done = f32[9216,128]{1,0:T(8,128)} async-done(((f32[1152,128]{1,0:T(8,128)}), f32[9216,128]{1,0:T(8,128)}) %all-gather.6.cloned.1.call-update) | async-done | bytes 4718608 | tf_op jit(solution)/shard_map/all_gather | solution.py:177
  (166 shorter events, 163.0 us)
Async XLA Ops:
  7.8 16.9 %all-to-all-start = ((s32[8,1,4]{2,1,0:T(1,128)}), s32[8,1,4]{2,1,0:T(1,128)S(1)}, u32[]{:S(2)}, u32[]{:S(2)}) async-start(s32[8,1,4]{2,1,0:T(1,128)} %broadcast_in_dim.67), calls=%async_computation | async-start | bytes 8192 | tf_op jit(solution)/shard_map/all_to_all | solution.py:153
  24.7 99.2 %all-to-all-start.1 = ((bf16[8,512,512]{2,1,0:T(8,128)(2,1)}), bf16[8,512,512]{2,1,0:T(8,128)(2,1)}, u32[]{:S(2)}, u32[]{:S(2)}) async-start(bf16[8,512,512]{2,1,0:T(8,128)(2,1)} %broadcast_select_fusion), calls=%async_computation.1 | async-start | bytes 8388608 | tf_op jit(solution)/shard_map/all_to_all | solution.py:152
  29.8 202.2 %reduce-scatter.4.cloned.1.call-start = ((), (), s32[]{:S(2)}) async-start(), calls=%async_computation.5 | async-start | bytes 4587520 | tf_op jit(solution)/shard_map/reduce_scatter | solution.py:171
  153.9 22.7 %copy-start.2 = (s32[55]{0:T(128)S(1)}, s32[55]{0:T(128)}, u32[]{:S(2)}) copy-start(s32[55]{0:T(128)} %constant.760) | copy-start | bytes 664
  182.0 129.7 %copy-start.3 = (s32[90]{0:T(128)S(1)}, s32[90]{0:T(128)}, u32[]{:S(2)}) copy-start(s32[90]{0:T(128)} %constant.761) | copy-start | bytes 1084
  186.4 71.1 %reduce-scatter.6.cloned.1.call-start = ((), (), s32[]{:S(2)}) async-start(), calls=%async_computation.6 | async-start | bytes 1146880 | tf_op jit(solution)/shard_map/reduce_scatter | solution.py:171
  232.0 53.2 %reduce-scatter.8.cloned.1.call-start = ((), (), s32[]{:S(2)}) async-start(), calls=%async_computation.7 | async-start | bytes 344064 | tf_op jit(solution)/shard_map/reduce_scatter | solution.py:171
  257.5 97.3 %all-gather.4.cloned.1.call-start = ((), (), s32[]{:S(2)}) async-start(), calls=%async_computation.8 | async-start | bytes 4587520 | tf_op jit(solution)/shard_map/all_gather | solution.py:174
  311.7 447.2 %all-gather.6.cloned.1.call-start = ((), (), s32[]{:S(2)}) async-start(), calls=%async_computation.9 | async-start | bytes 5308416 | tf_op jit(solution)/shard_map/all_gather | solution.py:177
  428.7 2.2 copy-start
  463.5 1.8 copy-start.1
Sparse Core Ops, SparseCore 0:
  186.5 45.4 reduce-scatter.3
  234.6 22.9 reduce-scatter.5
  260.0 25.1 reduce-scatter.7
  311.8 42.9 all-gather.3
  699.0 59.8 all-gather.5
where the time goes:
time: 780 us; the launch traced here: 771 us
  waiting for transfers between devices  295 us (38%)
  other arithmetic  256 us (33%)
  matrix products  85.5 us (11%)
  local copies, waits for them, and re-layouts  81.5 us (10%)
  blocking collectives  26.5 us (3%)
  between operations  14.3 us (2%)
  starting transfers between devices  11.2 us (1%)
    another operation x30, other arithmetic, _chol_inv(): lower = jnp.linalg.cholesky(block, symmetrize_input=False)  125 us
    another operation x15, other arithmetic, _chol_inv(): lax.linalg.triangular_solve(lower, eye, left_side=True, lower=True)  103 us
    reduce_scatter x3, waiting for transfers between devices, body(): mine = lax.psum_scatter(mine, axis, scatter_dimension=0, tiled=True)  98.6 us
    all_to_all x1, waiting for transfers between devices, body(): lax.all_to_all(ordered, 'owner', split_axis=0, concat_axis=1, tiled=True)  93.7 us
    all_gather x1, waiting for transfers between devices, body(): return lax.all_gather(results, 'owner', axis=0, tiled=True)  60 us
    dot_general x18, matrix products, _mm_nt(): lax.dot_general(a, b, (((1,), (1,)), ((), ())), precision=HIGH, preferred...  44.6 us
    all_gather x1, waiting for transfers between devices, body(): gathered = lax.all_gather(gathered, axis, axis=0, tiled=True)  43 us
    all_gather x2, blocking collectives, body(): gathered = lax.all_gather(gathered, axis, axis=0, tiled=True)  26.5 us
  transfers between devices with their start and end apart: 7, of which 6 were waited for; matrix products, arithmetic and copies ran while one was open for 1% of the time, Pallas kernels for 0%

commit v1 on v0

--- a/solution.py
+++ b/solution.py
@@ -174,7 +174,9 @@
         gathered = lax.all_gather(gathered, axis, axis=0, tiled=True)
     gathered = gathered.reshape(padded, block, block)
     results = precondition_blocks(gathered, nb, total_rows)[None]
-    return lax.all_gather(results, "owner", axis=0, tiled=True)
+    return jnp.concatenate(
+        lax.all_to_all(jnp.stack([results] * lax.axis_size("owner")), "owner", 0, 0), axis=0
+    )
 
 
 DP_AXES = ("dp_x", "dp_z", "dp_y")

time: 780 us -> 827 us (1.060)
  blocking collectives: 26.5 us -> 136 us
  waiting for transfers between devices: 295 us -> 235 us
    all_to_all x0 -> x1, blocking collectives: none -> 110 us  [body(): lax.all_to_all(jnp.stack([results] * lax.axis_size('owner')), 'owner', 0, 0)]
    all_gather x1 -> x0, waiting for transfers between devices: 60 us -> none  [body(): return lax.all_gather(results, 'owner', axis=0, tiled=True)]
  transfers between devices with their start and end apart: 7 -> 6, of which waited for: 6 -> 5; matrix products, arithmetic and copies ran while one was open for 1% -> 1% of each run, Pallas kernels for 0% -> 0%
where the time goes in v1:
time: 827 us; the launch traced here: 817 us
  other arithmetic  256 us (31%)
  waiting for transfers between devices  235 us (28%)
  blocking collectives  136 us (16%)
  matrix products  84.7 us (10%)
  local copies, waits for them, and re-layouts  79.2 us (10%)
  between operations  14.3 us (2%)
  starting transfers between devices  11.2 us (1%)
    another operation x30, other arithmetic, _chol_inv(): lower = jnp.linalg.cholesky(block, symmetrize_input=False)  125 us
    all_to_all x1, blocking collectives, body(): lax.all_to_all(jnp.stack([results] * lax.axis_size('owner')), 'owner', 0, 0)  110 us
    another operation x15, other arithmetic, _chol_inv(): lax.linalg.triangular_solve(lower, eye, left_side=True, lower=True)  103 us
    reduce_scatter x3, waiting for transfers between devices, body(): mine = lax.psum_scatter(mine, axis, scatter_dimension=0, tiled=True)  98.6 us
    all_to_all x1, waiting for transfers between devices, body(): lax.all_to_all(ordered, 'owner', split_axis=0, concat_axis=1, tiled=True)  93.7 us
    dot_general x18, matrix products, _mm_nt(): lax.dot_general(a, b, (((1,), (1,)), ((), ())), precision=HIGH, preferred...  44.6 us
    all_gather x1, waiting for transfers between devices, body(): gathered = lax.all_gather(gathered, axis, axis=0, tiled=True)  43.1 us
    all_gather x2, blocking collectives, body(): gathered = lax.all_gather(gathered, axis, axis=0, tiled=True)  26.5 us
  transfers between devices with their start and end apart: 6, of which 5 were waited for; matrix products, arithmetic and copies ran while one was open for 1% of the time, Pallas kernels for 0%

profile of v1, /device:TPU:2, one launch (start us, length us, event | category | flops | bytes accessed | tf_op | source)
XLA Modules:
  0.0 817.5 jit_solution(11178087590433460996)
XLA Ops:
  30.2 93.7 %all-to-all-done.1 = bf16[8,512,512]{2,1,0:T(8,128)(2,1)} async-done(((bf16[8,512,512]{2,1,0:T(8,128)(2,1)}), bf16[8,512,512]{2,1,0:T(8,128)(2,1)}, u32[]{:S(2)}, u32[]{:S(2)}) %all-to-all-start.1) | async-done | bytes 4194336 | tf_op jit(solution)/shard_map/all_to_all | solution.py:152
  139.5 14.3 %copy.37 = bf16[1280,4096]{1,0:T(8,128)(2,1)} copy(bf16[1280,4096]{0,1:T(8,128)(2,1)} %fusion) | data formatting | bytes 20971520 | tf_op jit(solution)/shard_map/dot_general | solution.py:158
  153.9 22.7 %convolution_bitcast_fusion = f32[10,10,128,128]{3,2,1,0:T(8,128)} fusion(bf16[10,128,4096,1]{2,1,3,0:T(8,128)(2,1)} %bitcast.177, bf16[10,128,4096,1]{2,1,0,3:T(8,128)(2,1)} %bitcast.178), kind=kOutput, calls=%fused_computation.13 | convolution fusion | flops 13421772800 | bytes 27525120 | tf_op jit(solution)/shard_map/dot_general | solution.py:158
  186.4 45.5 %reduce-scatter.4.cloned.1.call-done = f32[1792,128]{1,0:T(8,128)} async-done(((f32[7168,128]{1,0:T(8,128)}), f32[1792,128]{1,0:T(8,128)}) %reduce-scatter.4.cloned.1.call-update) | async-done | bytes 917520 | tf_op jit(solution)/shard_map/reduce_scatter | solution.py:171
  232.1 25.5 %reduce-scatter.6.cloned.1.call-done = f32[448,128]{1,0:T(8,128)} async-done(((f32[1792,128]{1,0:T(8,128)}), f32[448,128]{1,0:T(8,128)}) %reduce-scatter.6.cloned.1.call-update) | async-done | bytes 229392 | tf_op jit(solution)/shard_map/reduce_scatter | solution.py:171
  257.6 27.6 %reduce-scatter.8.cloned.1.call-done = f32[224,128]{1,0:T(8,128)} async-done(((f32[448,128]{1,0:T(8,128)}), f32[224,128]{1,0:T(8,128)}) %reduce-scatter.8.cloned.1.call-update) | async-done | bytes 114704 | tf_op jit(solution)/shard_map/reduce_scatter | solution.py:171
  285.2 12.2 %all_gather.9 = f32[448,128]{1,0:T(8,128)S(1)} all-gather(f32[224,128]{1,0:T(8,128)} %reduce-scatter.8.cloned.1.call-done), channel_id=1, replica_groups=mesh['dp_x'=4,'dp_z'=2,'dp_y'=4,'owner'=8] {'dp_z'}, dimensions={0}, use_global_device_ids=true | all-gather | bytes 344064 | tf_op jit(solution)/shard_map/all_gather | solution.py:174
  297.4 14.3 %all_gather.10 = f32[1792,128]{1,0:T(8,128)} all-gather(f32[448,128]{1,0:T(8,128)S(1)} %all_gather.9), channel_id=1, replica_groups=mesh['dp_x'=4,'dp_z'=2,'dp_y'=4,'owner'=8] {'dp_x'}, dimensions={0}, use_global_device_ids=true | all-gather | bytes 1146880 | tf_op jit(solution)/shard_map/all_gather | solution.py:174
  311.7 43.1 %all-gather.2.cloned.1.call-done = f32[7168,128]{1,0:T(8,128)} async-done(((f32[1792,128]{1,0:T(8,128)}), f32[7168,128]{1,0:T(8,128)}) %all-gather.2.cloned.1.call-update) | async-done | bytes 3670032 | tf_op jit(solution)/shard_map/all_gather | solution.py:174
  366.6 9.8 %copy.38 = f32[10,128,9,128]{1,0,3,2:T(8,128)} copy(f32[10,128,9,128]{3,1,2,0:T(8,128)} %bitcast.171) | data formatting | bytes 11796480 | tf_op jit(solution)/shard_map/mul | solution.py:107
  376.5 9.2 %copy.61 = f32[144,8,10,128]{3,1,2,0:T(8,128)} copy(f32[144,8,10,128]{3,2,1,0:T(8,128)} %bitcast.168) | data formatting | bytes 11796480
  394.2 11.7 %cholesky.165 = f32[128,128]{1,0:T(8,128)S(1)} custom-call(f32[128,128]{1,0:T(8,128)S(1)} %select_add_fusion.9), custom_call_target="Cholesky" | custom-call | tf_op jit(solution)/shard_map/jit(cholesky)/cholesky | solution.py:92
  407.9 9.8 %custom-call.16 = f32[1,128,128]{1,2,0:T(8,128)S(1)} custom-call(f32[1,128,128]{2,1,0:T(8,128)S(1)} %get-tuple-element.334), custom_call_target="InvertDiagBlocksLowerTriangular" | custom-call | tf_op jit(solution)/shard_map/triangular_solve/custom-call.0 | solution.py:94
  430.9 11.7 %cholesky.176 = f32[128,128]{1,0:T(8,128)S(1)} custom-call(f32[128,128]{1,0:T(8,128)S(1)} %select_add_fusion.8), custom_call_target="Cholesky" | custom-call | tf_op jit(solution)/shard_map/jit(cholesky)/cholesky | solution.py:92
  444.7 9.8 %custom-call.17 = f32[1,128,128]{1,2,0:T(8,128)S(1)} custom-call(f32[1,128,128]{2,1,0:T(8,128)S(1)} %get-tuple-element.332), custom_call_target="InvertDiagBlocksLowerTriangular" | custom-call | tf_op jit(solution)/shard_map/triangular_solve/custom-call.0 | solution.py:94
  465.4 11.7 %cholesky.187 = f32[128,128]{1,0:T(8,128)S(1)} custom-call(f32[128,128]{1,0:T(8,128)S(1)} %select_add_fusion.7), custom_call_target="Cholesky" | custom-call | tf_op jit(solution)/shard_map/jit(cholesky)/cholesky | solution.py:92
  479.2 9.8 %custom-call.18 = f32[1,128,128]{1,2,0:T(8,128)S(1)} custom-call(f32[1,128,128]{2,1,0:T(8,128)S(1)} %get-tuple-element.330), custom_call_target="InvertDiagBlocksLowerTriangular" | custom-call | tf_op jit(solution)/shard_map/triangular_solve/custom-call.0 | solution.py:94
  497.5 11.9 %cholesky.198 = f32[128,128]{1,0:T(8,128)S(1)} custom-call(f32[128,128]{1,0:T(8,128)S(1)} %select_add_fusion.6), custom_call_target="Cholesky" | custom-call | tf_op jit(solution)/shard_map/jit(cholesky)/cholesky | solution.py:92
  511.3 9.8 %custom-call.19 = f32[1,128,128]{1,2,0:T(8,128)S(1)} custom-call(f32[1,128,128]{2,1,0:T(8,128)S(1)} %get-tuple-element.328), custom_call_target="InvertDiagBlocksLowerTriangular" | custom-call | tf_op jit(solution)/shard_map/triangular_solve/custom-call.0 | solution.py:94
  527.4 11.7 %cholesky.209 = f32[128,128]{1,0:T(8,128)S(1)} custom-call(f32[128,128]{1,0:T(8,128)S(1)} %select_add_fusion.5), custom_call_target="Cholesky" | custom-call | tf_op jit(solution)/shard_map/jit(cholesky)/cholesky | solution.py:92
  541.1 9.8 %custom-call.20 = f32[1,128,128]{1,2,0:T(8,128)S(1)} custom-call(f32[1,128,128]{2,1,0:T(8,128)S(1)} %get-tuple-element.326), custom_call_target="InvertDiagBlocksLowerTriangular" | custom-call | tf_op jit(solution)/shard_map/triangular_solve/custom-call.0 | solution.py:94
  556.6 11.7 %cholesky.220 = f32[128,128]{1,0:T(8,128)S(1)} custom-call(f32[128,128]{1,0:T(8,128)S(1)} %select_add_fusion.4), custom_call_target="Cholesky" | custom-call | tf_op jit(solution)/shard_map/jit(cholesky)/cholesky | solution.py:92
  570.2 9.8 %custom-call.21 = f32[1,128,128]{1,2,0:T(8,128)S(1)} custom-call(f32[1,128,128]{2,1,0:T(8,128)S(1)} %get-tuple-element.323), custom_call_target="InvertDiagBlocksLowerTriangular" | custom-call | tf_op jit(solution)/shard_map/triangular_solve/custom-call.0 | solution.py:94
  585.3 11.9 %cholesky.264 = f32[128,128]{1,0:T(8,128)S(1)} custom-call(f32[128,128]{1,0:T(8,128)S(1)} %select_add_fusion), custom_call_target="Cholesky" | custom-call | tf_op jit(solution)/shard_map/jit(cholesky)/cholesky | solution.py:92
  598.5 9.8 %custom-call.25 = f32[1,128,128]{1,2,0:T(8,128)S(1)} custom-call(f32[1,128,128]{2,1,0:T(8,128)S(1)} %fusion.72), custom_call_target="InvertDiagBlocksLowerTriangular" | custom-call | tf_op jit(solution)/shard_map/triangular_solve/custom-call.0 | solution.py:94
  608.6 11.7 %cholesky.231 = f32[128,128]{1,0:T(8,128)S(1)} custom-call(f32[128,128]{1,0:T(8,128)S(1)} %select_add_fusion.3), custom_call_target="Cholesky" | custom-call | tf_op jit(solution)/shard_map/jit(cholesky)/cholesky | solution.py:92
  622.3 9.8 %custom-call.22 = f32[1,128,128]{1,2,0:T(8,128)S(1)} custom-call(f32[1,128,128]{2,1,0:T(8,128)S(1)} %get-tuple-element.321), custom_call_target="InvertDiagBlocksLowerTriangular" | custom-call | tf_op jit(solution)/shard_map/triangular_solve/custom-call.0 | solution.py:94
  634.9 11.9 %cholesky.242 = f32[128,128]{1,0:T(8,128)S(1)} custom-call(f32[128,128]{1,0:T(8,128)S(1)} %select_add_fusion.2), custom_call_target="Cholesky" | custom-call | tf_op jit(solution)/shard_map/jit(cholesky)/cholesky | solution.py:92
  648.2 9.8 %custom-call.23 = f32[1,128,128]{1,2,0:T(8,128)S(1)} custom-call(f32[1,128,128]{2,1,0:T(8,128)S(1)} %fusion.70), custom_call_target="InvertDiagBlocksLowerTriangular" | custom-call | tf_op jit(solution)/shard_map/triangular_solve/custom-call.0 | solution.py:94
  658.9 11.7 %cholesky.253 = f32[128,128]{1,0:T(8,128)S(1)} custom-call(f32[128,128]{1,0:T(8,128)S(1)} %select_add_fusion.1), custom_call_target="Cholesky" | custom-call | tf_op jit(solution)/shard_map/jit(cholesky)/cholesky | solution.py:92
  671.9 9.8 %custom-call.24 = f32[1,128,128]{1,2,0:T(8,128)S(1)} custom-call(f32[1,128,128]{2,1,0:T(8,128)S(1)} %fusion.71), custom_call_target="InvertDiagBlocksLowerTriangular" | custom-call | tf_op jit(solution)/shard_map/triangular_solve/custom-call.0 | solution.py:94
  698.4 109.9 %all_to_all.23 = f32[8,1,1152,128]{3,2,1,0:T(8,128)S(1)} all-to-all(f32[8,1,1152,128]{3,2,1,0:T(8,128)S(1)} %stack.3), channel_id=1, replica_groups=mesh['dp_x'=4,'dp_z'=2,'dp_y'=4,'owner'=8] {'owner'}, dimensions={0} | all-to-all | bytes 9437184 | tf_op jit(solution)/shard_map/all_to_all | solution.py:178
  (165 shorter events, 159.7 us)
Async XLA Ops:
  7.8 16.9 %all-to-all-start = ((s32[8,1,4]{2,1,0:T(1,128)}), s32[8,1,4]{2,1,0:T(1,128)S(1)}, u32[]{:S(2)}, u32[]{:S(2)}) async-start(s32[8,1,4]{2,1,0:T(1,128)} %broadcast_in_dim.64), calls=%async_computation | async-start | bytes 8192 | tf_op jit(solution)/shard_map/all_to_all | solution.py:153
  24.7 99.2 %all-to-all-start.1 = ((bf16[8,512,512]{2,1,0:T(8,128)(2,1)}), bf16[8,512,512]{2,1,0:T(8,128)(2,1)}, u32[]{:S(2)}, u32[]{:S(2)}) async-start(bf16[8,512,512]{2,1,0:T(8,128)(2,1)} %broadcast_select_fusion), calls=%async_computation.1 | async-start | bytes 8388608 | tf_op jit(solution)/shard_map/all_to_all | solution.py:152
  29.8 202.2 %reduce-scatter.4.cloned.1.call-start = ((), (), s32[]{:S(2)}) async-start(), calls=%async_computation.6 | async-start | bytes 4587520 | tf_op jit(solution)/shard_map/reduce_scatter | solution.py:171
  153.9 22.7 %copy-start.2 = (s32[55]{0:T(128)S(1)}, s32[55]{0:T(128)}, u32[]{:S(2)}) copy-start(s32[55]{0:T(128)} %constant.760) | copy-start | bytes 664
  182.0 129.7 %copy-start.3 = (s32[90]{0:T(128)S(1)}, s32[90]{0:T(128)}, u32[]{:S(2)}) copy-start(s32[90]{0:T(128)} %constant.761) | copy-start | bytes 1084
  186.4 71.1 %reduce-scatter.6.cloned.1.call-start = ((), (), s32[]{:S(2)}) async-start(), calls=%async_computation.7 | async-start | bytes 1146880 | tf_op jit(solution)/shard_map/reduce_scatter | solution.py:171
  232.0 53.2 %reduce-scatter.8.cloned.1.call-start = ((), (), s32[]{:S(2)}) async-start(), calls=%async_computation.8 | async-start | bytes 344064 | tf_op jit(solution)/shard_map/reduce_scatter | solution.py:171
  257.5 97.3 %all-gather.2.cloned.1.call-start = ((), (), s32[]{:S(2)}) async-start(), calls=%async_computation.9 | async-start | bytes 4587520 | tf_op jit(solution)/shard_map/all_gather | solution.py:174
  428.7 2.2 copy-start
  463.5 1.8 copy-start.1
Sparse Core Ops, SparseCore 0:
  186.5 45.4 reduce-scatter.3
  234.6 22.9 reduce-scatter.5
  260.0 25.1 reduce-scatter.7
  311.8 42.9 all-gather.1
